TPU v7x, 128 devices: a whole 4x4x4 slice. The times are simulated.
128 devices in a mesh: space: 32 (over x, z, core), feat: 4 (over y).
Axes of the slice: x: 4, y: 4, z: 4, core: 2. Of those that a mesh axis runs over, the one named last changes fastest.
Arguments:
- inputs: bfloat16 [2, 96, 180, 1024], P(None, 'space', None, 'feat'), may hold values from -15 to 15
- cotangent: bfloat16 [2, 96, 180, 1024], P(None, 'space', None, 'feat'), may hold values from -6 to 6
- spec_w1: float32 [2, 8, 128, 128], P(None, 'feat'), may hold values from -0.375 to 0.375
- spec_b1: float32 [2, 1024], P(None, 'feat'), may hold values from -0.3 to 0.3
- spec_w2: float32 [2, 8, 128, 128], P(None, 'feat'), may hold values from -0.375 to 0.375
- spec_b2: float32 [2, 1024], P(None, 'feat'), may hold values from -0.3 to 0.3
- up_weight: bfloat16 [1024, 4096], P(None, 'feat'), may hold values from -0.1875 to 0.1875
- down_weight: bfloat16 [4096, 1024], P('feat'), may hold values from -0.09375 to 0.09375
Outputs:
- output: bfloat16 [2, 96, 180, 1024], P(None, 'space', None, 'feat')
- grad_input: bfloat16 [2, 96, 180, 1024], P(None, 'space', None, 'feat')
All inputs are finite; a program needn't handle non-finite values.
Results may differ from a plain program's by a relative error of at most 0.0102.
Values may be sent and summed in bfloat16 or wider, within the bound.
No kernel may reach another device: no remote copies, remote signals or barrier semaphores. Data moves between devices by JAX's collectives and lax.ppermute only.
A program may use at most 128 MiB of HBM per device.

v0:
```python
import math
import jax
import jax.numpy as jnp
from jax import lax
from jax.sharding import PartitionSpec as P

EPSILON = 1e-05
SHRINK_LEVEL = 0.1
HIGHEST = lax.Precision.HIGHEST


def longitude_tables(width_lon):
    mode_count = width_lon // 2 + 1
    cell_index = jnp.arange(width_lon, dtype=jnp.int32)[:, None]
    wave_number = jnp.arange(mode_count, dtype=jnp.int32)[None, :]
    phase_angle = (
        2.0 * math.pi / width_lon * (cell_index * wave_number % width_lon).astype(jnp.float32)
    )
    scaling = 1.0 / math.sqrt(width_lon)
    cos_fwd = jnp.cos(phase_angle) * scaling
    sin_fwd = -jnp.sin(phase_angle) * scaling
    doubled = jnp.where((wave_number == 0) | (wave_number * 2 == width_lon), 1.0, 2.0).astype(
        jnp.float32
    )
    return (cos_fwd, sin_fwd, cos_fwd * doubled, sin_fwd * doubled)


def padded_tables(width_lon, multiple):
    tables = longitude_tables(width_lon)
    modes = tables[0].shape[1]
    extra = -modes % multiple
    return tuple((jnp.pad(table, ((0, 0), (0, extra))) for table in tables))


def lat_apply(table, field):
    return jnp.einsum("gh,bhkc->bgkc", table, field, precision=HIGHEST)


def complex_latitude(table_cos, table_sin, real_part, imag_part, inverse):
    if inverse:
        return (
            lat_apply(table_cos, real_part) + lat_apply(table_sin, imag_part),
            lat_apply(table_cos, imag_part) - lat_apply(table_sin, real_part),
        )
    return (
        lat_apply(table_cos, real_part) - lat_apply(table_sin, imag_part),
        lat_apply(table_cos, imag_part) + lat_apply(table_sin, real_part),
    )


def lon_forward(field, table):
    return jnp.einsum("brwc,wk->brkc", field, table, precision=HIGHEST)


def lon_back(spec, table):
    return jnp.einsum("brkc,wk->brwc", spec, table, precision=HIGHEST)


def to_blocks(field, block_size):
    return field.reshape(field.shape[:-1] + (field.shape[-1] // block_size, block_size))


def block_mult(field, weights):
    return jnp.einsum("...nc,nce->...ne", field, weights, precision=HIGHEST)


def block_mult_back(field, weights):
    return jnp.einsum("...ne,nce->...nc", field, weights, precision=HIGHEST)


def block_product(real_part, imag_part, weights):
    return (
        block_mult(real_part, weights[0]) - block_mult(imag_part, weights[1]),
        block_mult(real_part, weights[1]) + block_mult(imag_part, weights[0]),
    )


def block_adjoint(real_part, imag_part, weights):
    return (
        block_mult_back(real_part, weights[0]) + block_mult_back(imag_part, weights[1]),
        block_mult_back(imag_part, weights[0]) - block_mult_back(real_part, weights[1]),
    )


def latitude_tables(length):
    index_row = jnp.arange(length, dtype=jnp.int32)
    phase_angle = (
        2.0
        * math.pi
        / length
        * (index_row[:, None] * index_row[None, :] % length).astype(jnp.float32)
    )
    scaling = 1.0 / math.sqrt(length)
    return (jnp.cos(phase_angle) * scaling, -jnp.sin(phase_angle) * scaling)


def to_columns(real_part, imag_part):
    stacked = jnp.stack([real_part, imag_part])
    moved = lax.all_to_all(stacked, "space", 3, 2, tiled=True)
    return (moved[0], moved[1])


def to_rows(real_part, imag_part):
    stacked = jnp.stack([real_part, imag_part])
    moved = lax.all_to_all(stacked, "space", 2, 3, tiled=True)
    return (moved[0], moved[1])


def enter_spectrum(real_part, imag_part):
    length = real_part.shape[1] * lax.axis_size("space")
    table_cos, table_sin = latitude_tables(length)
    real_part, imag_part = to_columns(real_part, imag_part)
    return complex_latitude(table_cos, table_sin, real_part, imag_part, False)


def leave_spectrum(real_part, imag_part):
    table_cos, table_sin = latitude_tables(real_part.shape[1])
    real_part, imag_part = complex_latitude(table_cos, table_sin, real_part, imag_part, True)
    return to_rows(real_part, imag_part)


def token_sums(first_term, second_term):
    pair = jnp.stack([first_term, second_term])
    count = lax.axis_size("feat")
    bit = 1
    while bit < count:
        pair = pair + lax.ppermute(pair, "feat", [(i, i ^ bit) for i in range(count)])
        bit *= 2
    return (pair[0], pair[1])


def ring_send(block):
    count = lax.axis_size("feat")
    return [block] + [
        lax.ppermute(block, "feat", [(i, (i + shift) % count) for i in range(count)])
        for shift in range(1, count)
    ]


def ring_assemble(parts):
    count = len(parts)
    position = lax.axis_index("feat")
    block = parts[0]
    width = block.shape[-1]
    whole = jnp.zeros(block.shape[:-1] + (width * count,), block.dtype)
    for shift, moved in enumerate(parts):
        source = (position + count - shift) % count
        whole = lax.dynamic_update_slice_in_dim(whole, moved, source * width, axis=block.ndim - 1)
    return whole


def channel_share(term):
    return lax.psum_scatter(
        term.astype(jnp.bfloat16), "feat", scatter_dimension=3, tiled=True
    ).astype(jnp.float32)


def gelu_value(field):
    return 0.5 * field * (1.0 + lax.erf(field * (1.0 / math.sqrt(2.0))))


def gelu_slope(field):
    return 0.5 * (1.0 + lax.erf(field * (1.0 / math.sqrt(2.0)))) + field * jnp.exp(
        -0.5 * field * field
    ) * (1.0 / math.sqrt(2.0 * math.pi))


def spectral_forward(field, spec_w1, spec_b1, spec_w2, spec_b2, cos_fwd, sin_fwd):
    block_size = spec_w1.shape[2]
    spec_real, spec_imag = enter_spectrum(lon_forward(field, cos_fwd), lon_forward(field, sin_fwd))
    spec_shape = spec_real.shape
    bias_one = to_blocks(spec_b1, block_size)
    bias_two = to_blocks(spec_b2, block_size)
    first_real, first_imag = block_product(
        to_blocks(spec_real, block_size), to_blocks(spec_imag, block_size), spec_w1
    )
    first_real = jax.nn.relu(first_real + bias_one[0])
    first_imag = jax.nn.relu(first_imag + bias_one[1])
    second_real, second_imag = block_product(first_real, first_imag, spec_w2)
    second_real = second_real + bias_two[0]
    second_imag = second_imag + bias_two[1]
    shrunk_real = (second_real - jnp.clip(second_real, -SHRINK_LEVEL, SHRINK_LEVEL)).reshape(
        spec_shape
    )
    shrunk_imag = (second_imag - jnp.clip(second_imag, -SHRINK_LEVEL, SHRINK_LEVEL)).reshape(
        spec_shape
    )
    back = complex_latitude_inverse(shrunk_real, shrunk_imag)
    return (back, (first_real, first_imag, second_real, second_imag))


def complex_latitude_inverse(real_part, imag_part):
    table_cos, table_sin = latitude_tables(real_part.shape[1])
    return complex_latitude(table_cos, table_sin, real_part, imag_part, True)


def spectral_leave(back, cos_inv, sin_inv):
    back_real, back_imag = to_rows(*back)
    return lon_back(back_real, cos_inv) + lon_back(back_imag, sin_inv)


def spectral_backward(grad_field, saved, spec_w1, spec_w2, cos_fwd, sin_fwd, cos_inv, sin_inv):
    block_size = spec_w1.shape[2]
    first_real, first_imag, second_real, second_imag = saved
    grad_real, grad_imag = enter_spectrum(
        lon_forward(grad_field, cos_inv), lon_forward(grad_field, sin_inv)
    )
    spec_shape = grad_real.shape
    grad_real = jnp.where(
        jnp.abs(second_real) > SHRINK_LEVEL, to_blocks(grad_real, block_size), 0.0
    )
    grad_imag = jnp.where(
        jnp.abs(second_imag) > SHRINK_LEVEL, to_blocks(grad_imag, block_size), 0.0
    )
    first_grad_real, first_grad_imag = block_adjoint(grad_real, grad_imag, spec_w2)
    first_grad_real = jnp.where(first_real > 0.0, first_grad_real, 0.0)
    first_grad_imag = jnp.where(first_imag > 0.0, first_grad_imag, 0.0)
    spec_grad_real, spec_grad_imag = block_adjoint(first_grad_real, first_grad_imag, spec_w1)
    rows_real, rows_imag = leave_spectrum(
        spec_grad_real.reshape(spec_shape), spec_grad_imag.reshape(spec_shape)
    )
    return lon_back(rows_real, cos_fwd) + lon_back(rows_imag, sin_fwd)


def per_device(inputs, cotangent, spec_w1, spec_b1, spec_w2, spec_b2, up_weight, down_weight):
    full_width = up_weight.shape[0]
    block_size = spec_w1.shape[2]
    cos_fwd, sin_fwd, cos_inv, sin_inv = padded_tables(inputs.shape[2], lax.axis_size("space"))
    values = inputs.astype(jnp.float32)
    cotangent_parts = ring_send(cotangent)
    first_sum, second_sum = token_sums(jnp.sum(values, axis=-1), jnp.sum(values * values, axis=-1))
    mean_one = first_sum[..., None] / full_width
    rstd_one = lax.rsqrt(second_sum[..., None] / full_width - mean_one * mean_one + EPSILON)
    normed = (values - mean_one) * rstd_one
    block_count = spec_w1.shape[1]
    shrunk_parts, saved_parts = ([], [])
    for block in range(block_count):
        channels = slice(block * block_size, (block + 1) * block_size)
        shrunk, saved = spectral_forward(
            normed[..., channels],
            spec_w1[:, block : block + 1],
            spec_b1[:, channels],
            spec_w2[:, block : block + 1],
            spec_b2[:, channels],
            cos_fwd,
            sin_fwd,
        )
        shrunk_parts.append(shrunk)
        saved_parts.append(saved)
    shrunk_parts[-1], cotangent_parts = lax.optimization_barrier(
        (shrunk_parts[-1], cotangent_parts)
    )
    whole_cotangent = ring_assemble(cotangent_parts)
    filtered = jnp.concatenate(
        [spectral_leave(shrunk, cos_inv, sin_inv) for shrunk in shrunk_parts], axis=-1
    )
    residual = (filtered + normed + values).astype(jnp.bfloat16)
    residual_vals = residual.astype(jnp.float32)
    whole_residual = lax.all_gather(residual, "feat", axis=3, tiled=True)
    whole_vals = whole_residual.astype(jnp.float32)
    mean_two = jnp.sum(whole_vals, axis=-1, keepdims=True) / full_width
    square_two = jnp.sum(whole_vals * whole_vals, axis=-1, keepdims=True) / full_width
    rstd_two = lax.rsqrt(square_two - mean_two * mean_two + EPSILON)
    vhat = (whole_vals - mean_two) * rstd_two
    hidden = jnp.einsum(
        "brwd,dh->brwh", vhat.astype(jnp.bfloat16), up_weight, preferred_element_type=jnp.float32
    )
    activated = gelu_value(hidden).astype(jnp.bfloat16)
    mixed_term = jnp.einsum(
        "brwh,hd->brwd", activated, down_weight, preferred_element_type=jnp.float32
    )
    output = (residual_vals + channel_share(mixed_term)).astype(jnp.bfloat16)
    grad_act = jnp.einsum(
        "brwd,hd->brwh", whole_cotangent, down_weight, preferred_element_type=jnp.float32
    )
    grad_hidden = (grad_act * gelu_slope(hidden)).astype(jnp.bfloat16)
    grad_term = jnp.einsum(
        "brwh,dh->brwd", grad_hidden, up_weight, preferred_element_type=jnp.float32
    )
    total_one, total_two = token_sums(
        jnp.sum(grad_term, axis=-1), jnp.sum(grad_term * vhat, axis=-1)
    )
    grad_vhat = channel_share(grad_term)
    own_hat = (residual_vals - mean_two) * rstd_two
    grad_residual = cotangent.astype(jnp.float32) + rstd_two * (
        grad_vhat
        - total_one[..., None] / full_width
        - own_hat * (total_two[..., None] / full_width)
    )
    grad_filter = jnp.concatenate(
        [
            spectral_backward(
                grad_residual[..., block * block_size : (block + 1) * block_size],
                saved_parts[block],
                spec_w1[:, block : block + 1],
                spec_w2[:, block : block + 1],
                cos_fwd,
                sin_fwd,
                cos_inv,
                sin_inv,
            )
            for block in range(block_count)
        ],
        axis=-1,
    )
    grad_normed = grad_residual + grad_filter
    norm_one, norm_two = token_sums(
        jnp.sum(grad_normed, axis=-1), jnp.sum(grad_normed * normed, axis=-1)
    )
    grad_input = grad_residual + rstd_one * (
        grad_normed - norm_one[..., None] / full_width - normed * (norm_two[..., None] / full_width)
    )
    return (output, grad_input.astype(jnp.bfloat16))


def solution(mesh):
    return jax.shard_map(
        per_device,
        mesh=mesh,
        in_specs=(
            P(None, "space", None, "feat"),
            P(None, "space", None, "feat"),
            P(None, "feat", None, None),
            P(None, "feat"),
            P(None, "feat", None, None),
            P(None, "feat"),
            P(None, "feat"),
            P("feat", None),
        ),
        out_specs=(P(None, "space", None, "feat"), P(None, "space", None, "feat")),
        check_vma=False,
    )
```

profile of v0, /device:TPU:0, one launch (start us, length us, event | category | flops | bytes accessed | tf_op | source)
XLA Modules:
  0.0 356.5 jit_solution(820768273294857177)
XLA Ops:
  7.2 3.2 collective-permute-start.4
  13.5 2.0 collective-permute-start
  17.2 17.8 %collective-permute-done = f32[2,2,3,180]{3,2,1,0:T(4,128)S(1)} collective-permute-done((f32[2,2,3,180]{3,2,1,0:T(4,128)S(1)}, f32[2,2,3,180]{3,2,1,0:T(4,128)S(1)}, u32[]{:S(2)}, u32[]{:S(2)}) %collective-permute-start) | collective-permute-done | bytes 8672 | tf_op jit(solution)/shard_map/ppermute | solution.py:127
  35.0 3.1 collective-permute-start.1
  44.0 8.3 %all-to-all-start = ((f32[2,2,3,96,128]{4,1,2,0,3:T(2,128)}), f32[2,2,3,96,128]{4,1,2,0,3:T(2,128)}, u32[]{:S(2)}, u32[]{:S(2)}) async-start(f32[2,2,3,96,128]{4,1,2,0,3:T(2,128)} %copy.147), calls=%async_computation | async-start | bytes 1179648 | tf_op jit(solution)/shard_map/all_to_all | solution.py:99
  55.2 8.9 %all-to-all-done = f32[2,2,3,96,128]{4,1,2,0,3:T(2,128)} async-done(((f32[2,2,3,96,128]{4,1,2,0,3:T(2,128)}), f32[2,2,3,96,128]{4,1,2,0,3:T(2,128)}, u32[]{:S(2)}, u32[]{:S(2)}) %all-to-all-start) | async-done | bytes 589856 | tf_op jit(solution)/shard_map/all_to_all | solution.py:99
  64.1 4.6 %all-to-all-start.2 = ((f32[2,2,3,96,128]{4,1,2,0,3:T(2,128)}), f32[2,2,3,96,128]{4,1,2,0,3:T(2,128)S(1)}, u32[]{:S(2)}, u32[]{:S(2)}) async-start(f32[2,2,3,96,128]{4,1,2,0,3:T(2,128)} %copy.161), calls=%async_computation.2 | async-start | bytes 1179648 | tf_op jit(solution)/shard_map/all_to_all | solution.py:99
  77.1 3.0 all-to-all-done.2
  92.2 4.6 %all-to-all-start.1 = ((f32[2,2,96,3,128]{4,1,3,0,2:T(2,128)}), f32[2,2,96,3,128]{4,1,3,0,2:T(2,128)}, u32[]{:S(2)}, u32[]{:S(2)}) async-start(f32[2,2,96,3,128]{4,1,3,0,2:T(2,128)} %copy.155), calls=%async_computation.1 | async-start | bytes 1179648 | tf_op jit(solution)/shard_map/all_to_all | solution.py:105
  103.0 5.5 %all-to-all-done.1 = f32[2,2,96,3,128]{4,1,3,0,2:T(2,128)} async-done(((f32[2,2,96,3,128]{4,1,3,0,2:T(2,128)}), f32[2,2,96,3,128]{4,1,3,0,2:T(2,128)}, u32[]{:S(2)}, u32[]{:S(2)}) %all-to-all-start.1) | async-done | bytes 589856 | tf_op jit(solution)/shard_map/all_to_all | solution.py:105
  108.5 4.1 %all-to-all-start.3 = ((f32[2,2,96,3,128]{4,1,3,0,2:T(2,128)}), f32[2,2,96,3,128]{4,1,3,0,2:T(2,128)S(1)}, u32[]{:S(2)}, u32[]{:S(2)}) async-start(f32[2,2,96,3,128]{4,1,3,0,2:T(2,128)} %copy.169), calls=%async_computation.3 | async-start | bytes 1179648 | tf_op jit(solution)/shard_map/all_to_all | solution.py:105
  115.6 8.9 %all-to-all-done.3 = f32[2,2,96,3,128]{4,1,3,0,2:T(2,128)S(1)} async-done(((f32[2,2,96,3,128]{4,1,3,0,2:T(2,128)}), f32[2,2,96,3,128]{4,1,3,0,2:T(2,128)S(1)}, u32[]{:S(2)}, u32[]{:S(2)}) %all-to-all-start.3) | async-done | bytes 589856 | tf_op jit(solution)/shard_map/all_to_all | solution.py:105
  137.9 26.5 %all-gather.2.cloned.1.call-done = bf16[2,3,180,1024]{3,2,1,0:T(8,128)(2,1)} async-done(((bf16[2,3,180,256]{3,2,1,0:T(8,128)(2,1)}), bf16[2,3,180,1024]{3,2,1,0:T(8,128)(2,1)}) %all-gather.2.cloned.1.call-update) | async-done | bytes 2211856 | tf_op jit(solution)/shard_map/all_gather | solution.py:259
  164.5 2.5 convert_reduce_fusion
  167.1 5.0 %fusion.14 = f32[2,3,180,1024]{3,2,1,0:T(8,128)} fusion(bf16[2,3,180,1024]{3,2,1,0:T(8,128)(2,1)S(1)} %copy-done.32, f32[2,3,180]{2,1,0:T(4,128)S(1)} %get-tuple-element.54, f32[2,3,180]{2,1,0:T(4,128)S(1)} %get-tuple-element.53, bf16[1024,1024]{1,0:T(8,128)(2,1)S(1)} %copy-done), kind=kOutput, calls=%fused_computation.19 | convolution fusion | flops 2269347840 | bytes 8741312 | tf_op jit(solution)/shard_map/brwd,dh->brwh/dot_general | solution.py:265
  172.1 11.0 %fusion.552 = (f32[2,3,180]{2,1,0:T(4,128)S(1)}, f32[2,3,180]{2,1,0:T(4,128)S(1)}, bf16[2,3,180,1024]{3,2,1,0:T(8,128)(2,1)}) fusion(f32[2,3,180]{2,1,0:T(4,128)S(1)} %get-tuple-element.54, f32[2,3,180]{2,1,0:T(4,128)S(1)} %get-tuple-element.53, bf16[2,3,180,1024]{3,2,1,0:T(8,128)(2,1)} %all-gather.2.cloned.1.call-done, ...), kind=kOutput, calls=%fused_computation.644 | convolution fusion | flops 4548646912 | bytes 15270784 | tf_op jit(solution)/shard_map/brwh,dh->brwd/dot_general | solution.py:277
  184.7 6.2 %fusion.27 = bf16[2,3,180,1024]{3,2,1,0:T(8,128)(2,1)} fusion(bf16[1024,1024]{1,0:T(8,128)(2,1)S(1)} %copy-done.45, f32[2,3,180,1024]{3,2,1,0:T(8,128)} %fusion.14), kind=kOutput, calls=%fused_computation.35 | convolution fusion | flops 2271559680 | bytes 8732672 | tf_op jit(solution)/shard_map/brwh,hd->brwd/dot_general | solution.py:269
  191.8 2.9 collective-permute-done.5
  194.7 2.8 collective-permute-start.6
  197.5 2.9 collective-permute-done.6
  200.4 15.2 %reduce-scatter.5.cloned.1.call-done = bf16[2,3,180,256]{3,2,1,0:T(8,128)(2,1)} async-done(((bf16[2,3,180,1024]{3,2,1,0:T(8,128)(2,1)}), bf16[2,3,180,256]{3,2,1,0:T(8,128)(2,1)}) %reduce-scatter.5.cloned.1.call-update) | async-done | bytes 552976 | tf_op jit(solution)/shard_map/reduce_scatter | solution.py:153
  215.6 33.3 %reduce-scatter.3.cloned.1.call-done = bf16[2,3,180,256]{3,2,1,0:T(8,128)(2,1)} async-done(((bf16[2,3,180,1024]{3,2,1,0:T(8,128)(2,1)}), bf16[2,3,180,256]{3,2,1,0:T(8,128)(2,1)}) %reduce-scatter.3.cloned.1.call-update) | async-done | bytes 552976 | tf_op jit(solution)/shard_map/reduce_scatter | solution.py:153
  249.0 2.5 fusion.99
  253.7 7.6 %all-to-all-start.6 = ((f32[2,2,3,96,128]{4,1,2,0,3:T(2,128)}), f32[2,2,3,96,128]{4,1,2,0,3:T(2,128)S(1)}, u32[]{:S(2)}, u32[]{:S(2)}) async-start(f32[2,2,3,96,128]{4,1,2,0,3:T(2,128)} %copy.194), calls=%async_computation.8 | async-start | bytes 1179648 | tf_op jit(solution)/shard_map/all_to_all | solution.py:99
  263.7 9.5 %all-to-all-done.6 = f32[2,2,3,96,128]{4,1,2,0,3:T(2,128)S(1)} async-done(((f32[2,2,3,96,128]{4,1,2,0,3:T(2,128)}), f32[2,2,3,96,128]{4,1,2,0,3:T(2,128)S(1)}, u32[]{:S(2)}, u32[]{:S(2)}) %all-to-all-start.6) | async-done | bytes 589856 | tf_op jit(solution)/shard_map/all_to_all | solution.py:99
  273.2 4.1 %all-to-all-start.4 = ((f32[2,2,3,96,128]{4,1,2,0,3:T(2,128)}), f32[2,2,3,96,128]{4,1,2,0,3:T(2,128)S(1)}, u32[]{:S(2)}, u32[]{:S(2)}) async-start(f32[2,2,3,96,128]{4,1,2,0,3:T(2,128)} %copy.180), calls=%async_computation.6 | async-start | bytes 1179648 | tf_op jit(solution)/shard_map/all_to_all | solution.py:99
  278.6 10.6 %all-to-all-done.4 = f32[2,2,3,96,128]{4,1,2,0,3:T(2,128)S(1)} async-done(((f32[2,2,3,96,128]{4,1,2,0,3:T(2,128)}), f32[2,2,3,96,128]{4,1,2,0,3:T(2,128)S(1)}, u32[]{:S(2)}, u32[]{:S(2)}) %all-to-all-start.4) | async-done | bytes 589856 | tf_op jit(solution)/shard_map/all_to_all | solution.py:99
  299.7 4.9 %all-to-all-start.5 = ((f32[2,2,96,3,128]{4,1,3,0,2:T(2,128)}), f32[2,2,96,3,128]{4,1,3,0,2:T(2,128)}, u32[]{:S(2)}, u32[]{:S(2)}) async-start(f32[2,2,96,3,128]{4,1,3,0,2:T(2,128)} %copy.188), calls=%async_computation.7 | async-start | bytes 1179648 | tf_op jit(solution)/shard_map/all_to_all | solution.py:105
  316.4 6.9 %all-to-all-start.7 = ((f32[2,2,96,3,128]{4,1,3,0,2:T(2,128)}), f32[2,2,96,3,128]{4,1,3,0,2:T(2,128)S(1)}, u32[]{:S(2)}, u32[]{:S(2)}) async-start(f32[2,2,96,3,128]{4,1,3,0,2:T(2,128)} %copy.202), calls=%async_computation.9 | async-start | bytes 1179648 | tf_op jit(solution)/shard_map/all_to_all | solution.py:105
  325.6 9.5 %all-to-all-done.7 = f32[2,2,96,3,128]{4,1,3,0,2:T(2,128)S(1)} async-done(((f32[2,2,96,3,128]{4,1,3,0,2:T(2,128)}), f32[2,2,96,3,128]{4,1,3,0,2:T(2,128)S(1)}, u32[]{:S(2)}, u32[]{:S(2)}) %all-to-all-start.7) | async-done | bytes 589856 | tf_op jit(solution)/shard_map/all_to_all | solution.py:105
  338.8 3.5 collective-permute-done.7
  345.1 2.6 collective-permute-done.8
  (268 shorter events, 96.5 us)
Async XLA Ops:
  7.2 159.9 %copy-start = (bf16[1024,1024]{1,0:T(8,128)(2,1)S(1)}, bf16[1024,1024]{1,0:T(8,128)(2,1)}, u32[]{:S(2)}) copy-start(bf16[1024,1024]{1,0:T(8,128)(2,1)} %param.14) | copy-start | bytes 6291460
  7.2 94.4 %collective-permute-start.4 = (bf16[2,3,180,256]{3,0,2,1:T(2,128)(2,1)}, bf16[2,3,180,256]{3,0,2,1:T(2,128)(2,1)}, u32[]{:S(2)}, u32[]{:S(2)}) collective-permute-start(bf16[2,3,180,256]{3,0,2,1:T(2,128)(2,1)} %param.9), channel_id=1, source_target_pairs={{0,3},{1,0},{2,1},{3,2},{4,7},{5,4},{6,5},{7,6},{8,11},{9,8},{10,9... | collective-permute-start | bytes 1658888 | tf_op jit(solution)/shard_map/ppermute | solution.py:135
  10.3 91.3 %collective-permute-start.3 = (bf16[2,3,180,256]{3,0,2,1:T(2,128)(2,1)}, bf16[2,3,180,256]{3,0,2,1:T(2,128)(2,1)}, u32[]{:S(2)}, u32[]{:S(2)}) collective-permute-start(bf16[2,3,180,256]{3,0,2,1:T(2,128)(2,1)} %param.9), channel_id=1, source_target_pairs={{0,2},{1,3},{2,0},{3,1},{4,6},{5,7},{6,4},{7,5},{8,10},{9,11},{10,... | collective-permute-start | bytes 1658888 | tf_op jit(solution)/shard_map/ppermute | solution.py:135
  11.0 90.7 %collective-permute-start.2 = (bf16[2,3,180,256]{3,0,2,1:T(2,128)(2,1)}, bf16[2,3,180,256]{3,0,2,1:T(2,128)(2,1)}, u32[]{:S(2)}, u32[]{:S(2)}) collective-permute-start(bf16[2,3,180,256]{3,0,2,1:T(2,128)(2,1)} %param.9), channel_id=1, source_target_pairs={{0,1},{1,2},{2,3},{3,0},{4,5},{5,6},{6,7},{7,4},{8,9},{9,10},{10,1... | collective-permute-start | bytes 1658888 | tf_op jit(solution)/shard_map/ppermute | solution.py:135
  13.5 21.4 %collective-permute-start = (f32[2,2,3,180]{3,2,1,0:T(4,128)S(1)}, f32[2,2,3,180]{3,2,1,0:T(4,128)S(1)}, u32[]{:S(2)}, u32[]{:S(2)}) collective-permute-start(f32[2,2,3,180]{3,2,1,0:T(4,128)S(1)} %pad_maximum_fusion.8), channel_id=1, source_target_pairs={{0,1},{1,0},{2,3},{3,2},{4,5},{5,4},{6,7},{7,6},{8,9},{9,8},{10,11... | collective-permute-start | bytes 25928 | tf_op jit(solution)/shard_map/ppermute | solution.py:127
  17.1 35.8 %copy-start.23 = (f32[180,91]{1,0:T(8,128)}, f32[180,91]{1,0:T(8,128)S(1)}, u32[]{:S(2)}) copy-start(f32[180,91]{1,0:T(8,128)S(1)} %fusion.232) | copy-start | bytes 196564
  35.0 5.3 %collective-permute-start.1 = (f32[2,2,3,180]{3,2,1,0:T(4,128)S(1)}, f32[2,2,3,180]{3,2,1,0:T(4,128)S(1)}, u32[]{:S(2)}, u32[]{:S(2)}) collective-permute-start(f32[2,2,3,180]{3,2,1,0:T(4,128)S(1)} %fusion.551), channel_id=1, source_target_pairs={{0,2},{1,3},{2,0},{3,1},{4,6},{5,7},{6,4},{7,5},{8,10},{9,11},{10,... | collective-permute-start | bytes 25928 | tf_op jit(solution)/shard_map/ppermute | solution.py:127
  38.5 14.9 %copy-start.25 = (f32[180,91]{1,0:T(8,128)}, f32[180,91]{1,0:T(8,128)S(1)}, u32[]{:S(2)}) copy-start(f32[180,91]{1,0:T(8,128)S(1)} %fusion.228) | copy-start | bytes 196564
  42.2 10.1 %copy-start.44 = (f32[2,256]{1,0:T(2,128)S(1)}, f32[2,256]{1,0:T(2,128)}, u32[]{:S(2)}) copy-start(f32[2,256]{1,0:T(2,128)} %param.13) | copy-start | bytes 6148
  44.0 20.1 %all-to-all-start = ((f32[2,2,3,96,128]{4,1,2,0,3:T(2,128)}), f32[2,2,3,96,128]{4,1,2,0,3:T(2,128)}, u32[]{:S(2)}, u32[]{:S(2)}) async-start(f32[2,2,3,96,128]{4,1,2,0,3:T(2,128)} %copy.147), calls=%async_computation | async-start | bytes 1179648 | tf_op jit(solution)/shard_map/all_to_all | solution.py:99
  64.1 16.0 %all-to-all-start.2 = ((f32[2,2,3,96,128]{4,1,2,0,3:T(2,128)}), f32[2,2,3,96,128]{4,1,2,0,3:T(2,128)S(1)}, u32[]{:S(2)}, u32[]{:S(2)}) async-start(f32[2,2,3,96,128]{4,1,2,0,3:T(2,128)} %copy.161), calls=%async_computation.2 | async-start | bytes 1179648 | tf_op jit(solution)/shard_map/all_to_all | solution.py:99
  92.2 16.4 %all-to-all-start.1 = ((f32[2,2,96,3,128]{4,1,3,0,2:T(2,128)}), f32[2,2,96,3,128]{4,1,3,0,2:T(2,128)}, u32[]{:S(2)}, u32[]{:S(2)}) async-start(f32[2,2,96,3,128]{4,1,3,0,2:T(2,128)} %copy.155), calls=%async_computation.1 | async-start | bytes 1179648 | tf_op jit(solution)/shard_map/all_to_all | solution.py:105
  108.5 16.0 %all-to-all-start.3 = ((f32[2,2,96,3,128]{4,1,3,0,2:T(2,128)}), f32[2,2,96,3,128]{4,1,3,0,2:T(2,128)S(1)}, u32[]{:S(2)}, u32[]{:S(2)}) async-start(f32[2,2,96,3,128]{4,1,3,0,2:T(2,128)} %copy.169), calls=%async_computation.3 | async-start | bytes 1179648 | tf_op jit(solution)/shard_map/all_to_all | solution.py:105
  112.7 51.8 %all-gather.2.cloned.1.call-start = ((), (), s32[]{:S(2)}) async-start(), calls=%async_computation.10 | async-start | bytes 2826240 | tf_op jit(solution)/shard_map/all_gather | solution.py:259
  113.2 12.9 %copy-start.27 = (f32[180,91]{1,0:T(8,128)}, f32[180,91]{1,0:T(8,128)S(1)}, u32[]{:S(2)}) copy-start(f32[180,91]{1,0:T(8,128)S(1)} %get-tuple-element.64) | copy-start | bytes 196564
  113.2 14.1 %copy-start.29 = (f32[180,91]{1,0:T(8,128)}, f32[180,91]{1,0:T(8,128)S(1)}, u32[]{:S(2)}) copy-start(f32[180,91]{1,0:T(8,128)S(1)} %get-tuple-element.63) | copy-start | bytes 196564
  129.2 86.4 %reduce-scatter.5.cloned.1.call-start = ((), (), s32[]{:S(2)}) async-start(), calls=%async_computation.12 | async-start | bytes 2826240 | tf_op jit(solution)/shard_map/reduce_scatter | solution.py:153
  183.1 65.8 %reduce-scatter.3.cloned.1.call-start = ((), (), s32[]{:S(2)}) async-start(), calls=%async_computation.11 | async-start | bytes 2826240 | tf_op jit(solution)/shard_map/reduce_scatter | solution.py:153
  190.9 58.1 %copy-start.4 = (bf16[2,3,180,256]{3,2,1,0:T(8,128)(2,1)S(1)}, bf16[2,3,180,256]{3,2,1,0:T(8,128)(2,1)}, u32[]{:S(2)}) copy-start(bf16[2,3,180,256]{3,2,1,0:T(8,128)(2,1)} %fusion.102) | copy-start | bytes 1658884
  190.9 58.1 %copy-start.34 = (bf16[2,3,180,256]{3,0,2,1:T(2,128)(2,1)S(1)}, bf16[2,3,180,256]{3,0,2,1:T(2,128)(2,1)}, u32[]{:S(2)}) copy-start(bf16[2,3,180,256]{3,0,2,1:T(2,128)(2,1)} %param.9) | copy-start | bytes 1658884
  190.9 60.6 %copy-start.30 = (f32[180,91]{1,0:T(8,128)S(1)}, f32[180,91]{1,0:T(8,128)}, u32[]{:S(2)}) copy-start(f32[180,91]{1,0:T(8,128)} %copy-done.29) | copy-start | bytes 196564
  190.9 3.8 %collective-permute-start.5 = (f32[2,2,3,180]{3,2,1,0:T(4,128)S(1)}, f32[2,2,3,180]{3,2,1,0:T(4,128)S(1)}, u32[]{:S(2)}, u32[]{:S(2)}) collective-permute-start(f32[2,2,3,180]{3,2,1,0:T(4,128)S(1)} %pad_maximum_fusion.9), channel_id=1, source_target_pairs={{0,1},{1,0},{2,3},{3,2},{4,5},{5,4},{6,7},{7,6},{8,9},{9,8},{10,11... | collective-permute-start | bytes 25928 | tf_op jit(solution)/shard_map/ppermute | solution.py:127
  194.7 5.6 %collective-permute-start.6 = (f32[2,2,3,180]{3,2,1,0:T(4,128)S(1)}, f32[2,2,3,180]{3,2,1,0:T(4,128)S(1)}, u32[]{:S(2)}, u32[]{:S(2)}) collective-permute-start(f32[2,2,3,180]{3,2,1,0:T(4,128)S(1)} %fusion.550), channel_id=1, source_target_pairs={{0,2},{1,3},{2,0},{3,1},{4,6},{5,7},{6,4},{7,5},{8,10},{9,11},{10,... | collective-permute-start | bytes 25928 | tf_op jit(solution)/shard_map/ppermute | solution.py:127
  253.7 19.5 %all-to-all-start.6 = ((f32[2,2,3,96,128]{4,1,2,0,3:T(2,128)}), f32[2,2,3,96,128]{4,1,2,0,3:T(2,128)S(1)}, u32[]{:S(2)}, u32[]{:S(2)}) async-start(f32[2,2,3,96,128]{4,1,2,0,3:T(2,128)} %copy.194), calls=%async_computation.8 | async-start | bytes 1179648 | tf_op jit(solution)/shard_map/all_to_all | solution.py:99
  273.2 15.9 %all-to-all-start.4 = ((f32[2,2,3,96,128]{4,1,2,0,3:T(2,128)}), f32[2,2,3,96,128]{4,1,2,0,3:T(2,128)S(1)}, u32[]{:S(2)}, u32[]{:S(2)}) async-start(f32[2,2,3,96,128]{4,1,2,0,3:T(2,128)} %copy.180), calls=%async_computation.6 | async-start | bytes 1179648 | tf_op jit(solution)/shard_map/all_to_all | solution.py:99
  278.5 12.5 %copy-start.18 = (f32[2,96,3,1,128]{4,1,2,0,3:T(8,128)S(1)}, f32[2,96,3,1,128]{4,1,2,0,3:T(8,128)}, u32[]{:S(2)}) copy-start(f32[2,96,3,1,128]{4,1,2,0,3:T(8,128)} %copy-done.17) | copy-start | bytes 884740
  299.7 16.7 %all-to-all-start.5 = ((f32[2,2,96,3,128]{4,1,3,0,2:T(2,128)}), f32[2,2,96,3,128]{4,1,3,0,2:T(2,128)}, u32[]{:S(2)}, u32[]{:S(2)}) async-start(f32[2,2,96,3,128]{4,1,3,0,2:T(2,128)} %copy.188), calls=%async_computation.7 | async-start | bytes 1179648 | tf_op jit(solution)/shard_map/all_to_all | solution.py:105
  315.5 9.5 %copy-start.26 = (f32[180,91]{1,0:T(8,128)S(1)}, f32[180,91]{1,0:T(8,128)}, u32[]{:S(2)}) copy-start(f32[180,91]{1,0:T(8,128)} %copy-done.25) | copy-start | bytes 196564
  316.4 18.8 %all-to-all-start.7 = ((f32[2,2,96,3,128]{4,1,3,0,2:T(2,128)}), f32[2,2,96,3,128]{4,1,3,0,2:T(2,128)S(1)}, u32[]{:S(2)}, u32[]{:S(2)}) async-start(f32[2,2,96,3,128]{4,1,3,0,2:T(2,128)} %copy.202), calls=%async_computation.9 | async-start | bytes 1179648 | tf_op jit(solution)/shard_map/all_to_all | solution.py:105
  325.6 10.8 %copy-start.24 = (f32[180,91]{1,0:T(8,128)S(1)}, f32[180,91]{1,0:T(8,128)}, u32[]{:S(2)}) copy-start(f32[180,91]{1,0:T(8,128)} %copy-done.23) | copy-start | bytes 196564
  338.5 3.8 %collective-permute-start.7 = (f32[2,2,3,180]{3,2,1,0:T(4,128)S(1)}, f32[2,2,3,180]{3,2,1,0:T(4,128)S(1)}, u32[]{:S(2)}, u32[]{:S(2)}) collective-permute-start(f32[2,2,3,180]{3,2,1,0:T(4,128)S(1)} %pad_maximum_fusion.10), channel_id=1, source_target_pairs={{0,1},{1,0},{2,3},{3,2},{4,5},{5,4},{6,7},{7,6},{8,9},{9,8},{10,11... | collective-permute-start | bytes 25928 | tf_op jit(solution)/shard_map/ppermute | solution.py:127
  342.3 5.3 %collective-permute-start.8 = (f32[2,2,3,180]{3,2,1,0:T(4,128)S(1)}, f32[2,2,3,180]{3,2,1,0:T(4,128)S(1)}, u32[]{:S(2)}, u32[]{:S(2)}) collective-permute-start(f32[2,2,3,180]{3,2,1,0:T(4,128)S(1)} %fusion.549), channel_id=1, source_target_pairs={{0,2},{1,3},{2,0},{3,1},{4,6},{5,7},{6,4},{7,5},{8,10},{9,11},{10,... | collective-permute-start | bytes 25928 | tf_op jit(solution)/shard_map/ppermute | solution.py:127
  (34 other events, 106.2 us)
Sparse Core Ops, SparseCore 0:
  129.3 35.1 all-gather.1
  183.2 32.3 reduce-scatter.4
  218.2 30.7 reduce-scatter.2
where the time goes:
time: 363 us; the launch traced here: 356 us
  waiting for transfers between devices  163 us (45%)
  matrix products  68.6 us (19%)
  starting transfers between devices  61 us (17%)
  local copies, waits for them, and re-layouts  35.2 us (10%)
  between operations  15.7 us (4%)
  other arithmetic  12.5 us (3%)
    reduce_scatter x2, waiting for transfers between devices, channel_share(): lax.psum_scatter(term.astype(jnp.bfloat16), 'feat', scatter_dimension=3,...  48.5 us
    all_to_all x4, waiting for transfers between devices, to_columns(): moved = lax.all_to_all(stacked, 'space', 3, 2, tiled=True)  32 us
    ppermute x6, waiting for transfers between devices, token_sums(): lax.ppermute(pair, 'feat', [(i, i ^ bit) for i in range(count)])  31.4 us
    all_gather x1, waiting for transfers between devices, per_device(): whole_residual = lax.all_gather(residual, 'feat', axis=3, tiled=True)  26.5 us
    all_to_all x4, waiting for transfers between devices, to_rows(): moved = lax.all_to_all(stacked, 'space', 2, 3, tiled=True)  24.9 us
    all_to_all x4, starting transfers between devices, to_columns(): moved = lax.all_to_all(stacked, 'space', 3, 2, tiled=True)  24.7 us
    dot_general x32, matrix products, lat_apply(): return jnp.einsum('gh,bhkc->bgkc', table, field, precision=HIGHEST)  20.6 us
    all_to_all x4, starting transfers between devices, to_rows(): moved = lax.all_to_all(stacked, 'space', 2, 3, tiled=True)  20.6 us
  transfers between devices with their start and end apart: 20, of which 17 were waited for; matrix products, arithmetic and copies ran while one was open for 20% of the time, Pallas kernels for 0%

commit v1 on v0

--- a/solution.py
+++ b/solution.py
@@ -223,6 +223,14 @@
 
 
 def per_device(inputs, cotangent, spec_w1, spec_b1, spec_w2, spec_b2, up_weight, down_weight):
+
+    def proceed_the_sector(mat):
+        degree = lax.psum(1, axis_name="feat")
+        formed = tuple((degree if h == 3 else 1 for h in range(mat.ndim)))
+        val2 = jnp.tile(mat, formed)
+        mid_arr = lax.all_to_all(val2, axis_name="feat", split_axis=3, concat_axis=3, tiled=True)
+        return mid_arr
+
     full_width = up_weight.shape[0]
     block_size = spec_w1.shape[2]
     cos_fwd, sin_fwd, cos_inv, sin_inv = padded_tables(inputs.shape[2], lax.axis_size("space"))
@@ -256,7 +264,7 @@
     )
     residual = (filtered + normed + values).astype(jnp.bfloat16)
     residual_vals = residual.astype(jnp.float32)
-    whole_residual = lax.all_gather(residual, "feat", axis=3, tiled=True)
+    whole_residual = proceed_the_sector(residual)
     whole_vals = whole_residual.astype(jnp.float32)
     mean_two = jnp.sum(whole_vals, axis=-1, keepdims=True) / full_width
     square_two = jnp.sum(whole_vals * whole_vals, axis=-1, keepdims=True) / full_width

time: 363 us -> 382 us (1.052)
  local copies, waits for them, and re-layouts: 35.2 us -> 51 us
    all_to_all x0 -> x1, waiting for transfers between devices: none -> 30.4 us  [proceed_the_sector(): lax.all_to_all(val2, axis_name='feat', split_axis=3, concat_axis=3, tiled...]
    all_gather x1 -> x0, waiting for transfers between devices: 26.5 us -> none  [per_device(): whole_residual = lax.all_gather(residual, 'feat', axis=3, tiled=True)]
    all_to_all x0 -> x1, local copies, waits for them, and re-layouts: none -> 8.7 us  [proceed_the_sector(): lax.all_to_all(val2, axis_name='feat', split_axis=3, concat_axis=3, tiled...]
    reduce_scatter x2, waiting for transfers between devices: 48.5 us -> 42.9 us  [channel_share(): lax.psum_scatter(term.astype(jnp.bfloat16), 'feat', scatter_dimension=3,...]
    all_to_all x0 -> x1, starting transfers between devices: none -> 5.37 us  [proceed_the_sector(): lax.all_to_all(val2, axis_name='feat', split_axis=3, concat_axis=3, tiled...]
    another operation x0 -> x1, local copies, waits for them, and re-layouts: none -> 4.43 us  [proceed_the_sector(): val2 = jnp.tile(mat, formed)]
  transfers between devices with their start and end apart: 20 -> 20, of which waited for: 17 -> 17; matrix products, arithmetic and copies ran while one was open for 20% -> 19% of each run, Pallas kernels for 0% -> 0%
where the time goes in v1:
time: 382 us; the launch traced here: 375 us
  waiting for transfers between devices  163 us (43%)
  matrix products  68.6 us (18%)
  starting transfers between devices  64 us (17%)
  local copies, waits for them, and re-layouts  51 us (13%)
  between operations  15.9 us (4%)
  other arithmetic  11.7 us (3%)
    reduce_scatter x2, waiting for transfers between devices, channel_share(): lax.psum_scatter(term.astype(jnp.bfloat16), 'feat', scatter_dimension=3,...  42.9 us
    ppermute x6, waiting for transfers between devices, token_sums(): lax.ppermute(pair, 'feat', [(i, i ^ bit) for i in range(count)])  34 us
    all_to_all x4, waiting for transfers between devices, to_columns(): moved = lax.all_to_all(stacked, 'space', 3, 2, tiled=True)  31.3 us
    all_to_all x1, waiting for transfers between devices, proceed_the_sector(): lax.all_to_all(val2, axis_name='feat', split_axis=3, concat_axis=3, tiled...  30.4 us
    all_to_all x4, waiting for transfers between devices, to_rows(): moved = lax.all_to_all(stacked, 'space', 2, 3, tiled=True)  24.9 us
    all_to_all x4, starting transfers between devices, to_columns(): moved = lax.all_to_all(stacked, 'space', 3, 2, tiled=True)  24.7 us
    dot_general x32, matrix products, lat_apply(): return jnp.einsum('gh,bhkc->bgkc', table, field, precision=HIGHEST)  20.6 us
    all_to_all x4, starting transfers between devices, to_rows(): moved = lax.all_to_all(stacked, 'space', 2, 3, tiled=True)  20.6 us
  transfers between devices with their start and end apart: 20, of which 17 were waited for; matrix products, arithmetic and copies ran while one was open for 19% of the time, Pallas kernels for 0%

profile of v1, /device:TPU:0, one launch (start us, length us, event | category | flops | bytes accessed | tf_op | source)
XLA Modules:
  0.0 374.7 jit_solution(2184129439380494470)
XLA Ops:
  7.2 3.2 collective-permute-start.4
  17.2 17.8 %collective-permute-done = f32[2,2,3,180]{3,2,1,0:T(4,128)S(1)} collective-permute-done((f32[2,2,3,180]{3,2,1,0:T(4,128)S(1)}, f32[2,2,3,180]{3,2,1,0:T(4,128)S(1)}, u32[]{:S(2)}, u32[]{:S(2)}) %collective-permute-start) | collective-permute-done | bytes 8672 | tf_op jit(solution)/shard_map/ppermute | solution.py:127
  35.0 3.1 collective-permute-start.1
  44.0 8.3 %all-to-all-start = ((f32[2,2,3,96,128]{4,1,2,0,3:T(2,128)}), f32[2,2,3,96,128]{4,1,2,0,3:T(2,128)}, u32[]{:S(2)}, u32[]{:S(2)}) async-start(f32[2,2,3,96,128]{4,1,2,0,3:T(2,128)} %copy.149), calls=%async_computation | async-start | bytes 1179648 | tf_op jit(solution)/shard_map/all_to_all | solution.py:99
  55.2 8.9 %all-to-all-done = f32[2,2,3,96,128]{4,1,2,0,3:T(2,128)} async-done(((f32[2,2,3,96,128]{4,1,2,0,3:T(2,128)}), f32[2,2,3,96,128]{4,1,2,0,3:T(2,128)}, u32[]{:S(2)}, u32[]{:S(2)}) %all-to-all-start) | async-done | bytes 589856 | tf_op jit(solution)/shard_map/all_to_all | solution.py:99
  64.1 4.6 %all-to-all-start.2 = ((f32[2,2,3,96,128]{4,1,2,0,3:T(2,128)}), f32[2,2,3,96,128]{4,1,2,0,3:T(2,128)S(1)}, u32[]{:S(2)}, u32[]{:S(2)}) async-start(f32[2,2,3,96,128]{4,1,2,0,3:T(2,128)} %copy.163), calls=%async_computation.2 | async-start | bytes 1179648 | tf_op jit(solution)/shard_map/all_to_all | solution.py:99
  77.1 2.9 all-to-all-done.2
  92.2 4.6 %all-to-all-start.1 = ((f32[2,2,96,3,128]{4,1,3,0,2:T(2,128)}), f32[2,2,96,3,128]{4,1,3,0,2:T(2,128)}, u32[]{:S(2)}, u32[]{:S(2)}) async-start(f32[2,2,96,3,128]{4,1,3,0,2:T(2,128)} %copy.157), calls=%async_computation.1 | async-start | bytes 1179648 | tf_op jit(solution)/shard_map/all_to_all | solution.py:105
  103.0 5.5 %all-to-all-done.1 = f32[2,2,96,3,128]{4,1,3,0,2:T(2,128)} async-done(((f32[2,2,96,3,128]{4,1,3,0,2:T(2,128)}), f32[2,2,96,3,128]{4,1,3,0,2:T(2,128)}, u32[]{:S(2)}, u32[]{:S(2)}) %all-to-all-start.1) | async-done | bytes 589856 | tf_op jit(solution)/shard_map/all_to_all | solution.py:105
  108.5 4.1 %all-to-all-start.3 = ((f32[2,2,96,3,128]{4,1,3,0,2:T(2,128)}), f32[2,2,96,3,128]{4,1,3,0,2:T(2,128)S(1)}, u32[]{:S(2)}, u32[]{:S(2)}) async-start(f32[2,2,96,3,128]{4,1,3,0,2:T(2,128)} %copy.171), calls=%async_computation.3 | async-start | bytes 1179648 | tf_op jit(solution)/shard_map/all_to_all | solution.py:105
  115.5 8.9 %all-to-all-done.3 = f32[2,2,96,3,128]{4,1,3,0,2:T(2,128)S(1)} async-done(((f32[2,2,96,3,128]{4,1,3,0,2:T(2,128)}), f32[2,2,96,3,128]{4,1,3,0,2:T(2,128)S(1)}, u32[]{:S(2)}, u32[]{:S(2)}) %all-to-all-start.3) | async-done | bytes 589856 | tf_op jit(solution)/shard_map/all_to_all | solution.py:105
  130.2 4.4 %tile.4.clone = bf16[2,3,180,4,256]{2,0,1,4,3:T(2,128)(2,1)} broadcast(bf16[2,3,180,256]{2,0,1,3:T(2,128)(2,1)} %copy.232), dimensions={0,1,2,4} | broadcast | bytes 2764800 | tf_op jit(solution)/shard_map/tile | solution.py:230
  134.6 5.4 %all-to-all-start.4 = ((bf16[2,3,180,1024]{2,0,1,3:T(2,128)(2,1)}), bf16[2,3,180,1024]{2,0,1,3:T(2,128)(2,1)}, u32[]{:S(2)}, u32[]{:S(2)}) async-start(bf16[2,3,180,1024]{2,0,1,3:T(2,128)(2,1)} %bitcast.632), calls=%async_computation.4 | async-start | bytes 6291456 | tf_op jit(solution)/shard_map/all_to_all | solution.py:231
  148.5 30.4 %all-to-all-done.4 = bf16[2,3,180,1024]{2,0,1,3:T(2,128)(2,1)} async-done(((bf16[2,3,180,1024]{2,0,1,3:T(2,128)(2,1)}), bf16[2,3,180,1024]{2,0,1,3:T(2,128)(2,1)}, u32[]{:S(2)}, u32[]{:S(2)}) %all-to-all-start.4) | async-done | bytes 2211872 | tf_op jit(solution)/shard_map/all_to_all | solution.py:231
  178.9 8.7 %copy.178 = bf16[2,3,180,1024]{3,2,1,0:T(8,128)(2,1)} copy(bf16[2,3,180,1024]{2,0,1,3:T(2,128)(2,1)} %all-to-all-done.4) | data formatting | bytes 4423680 | tf_op jit(solution)/shard_map/all_to_all | solution.py:231
  187.6 2.5 convert_reduce_fusion
  190.1 5.0 %fusion.14 = f32[2,3,180,1024]{3,2,1,0:T(8,128)} fusion(bf16[2,3,180,1024]{3,2,1,0:T(8,128)(2,1)S(1)} %copy-done.4, f32[2,3,180]{2,1,0:T(4,128)S(1)} %get-tuple-element.54, f32[2,3,180]{2,1,0:T(4,128)S(1)} %get-tuple-element.53, bf16[1024,1024]{1,0:T(8,128)(2,1)S(1)} %copy-done), kind=kOutput, calls=%fused_computation.19 | convolution fusion | flops 2269347840 | bytes 8741312 | tf_op jit(solution)/shard_map/brwd,dh->brwh/dot_general | solution.py:273
  195.1 11.0 %fusion.552 = (f32[2,3,180]{2,1,0:T(4,128)S(1)}, f32[2,3,180]{2,1,0:T(4,128)S(1)}, bf16[2,3,180,1024]{3,2,1,0:T(8,128)(2,1)}) fusion(f32[2,3,180]{2,1,0:T(4,128)S(1)} %get-tuple-element.54, f32[2,3,180]{2,1,0:T(4,128)S(1)} %get-tuple-element.53, bf16[2,3,180,1024]{3,2,1,0:T(8,128)(2,1)} %copy.178, bf16[1024,1024]{1,0:T(8,128)(2,1)S(1)} %copy-done, ...), kind=kOutput, calls=%fused_computation.644 | convolution fusion | flops 4548646912 | bytes 15270784 | tf_op jit(solution)/shard_map/brwh,dh->brwd/dot_general | solution.py:285
  207.8 6.2 %fusion.27 = bf16[2,3,180,1024]{3,2,1,0:T(8,128)(2,1)} fusion(bf16[1024,1024]{1,0:T(8,128)(2,1)S(1)} %copy-done.47, f32[2,3,180,1024]{3,2,1,0:T(8,128)} %fusion.14), kind=kOutput, calls=%fused_computation.35 | convolution fusion | flops 2271559680 | bytes 8732672 | tf_op jit(solution)/shard_map/brwh,hd->brwd/dot_general | solution.py:277
  214.9 3.2 collective-permute-done.5
  218.8 5.2 %collective-permute-done.6 = f32[2,2,3,180]{3,2,1,0:T(4,128)S(1)} collective-permute-done((f32[2,2,3,180]{3,2,1,0:T(4,128)S(1)}, f32[2,2,3,180]{3,2,1,0:T(4,128)S(1)}, u32[]{:S(2)}, u32[]{:S(2)}) %collective-permute-start.6) | collective-permute-done | bytes 8672 | tf_op jit(solution)/shard_map/ppermute | solution.py:127
  224.0 9.5 %reduce-scatter.5.cloned.1.call-done = bf16[2,3,180,256]{3,2,1,0:T(8,128)(2,1)} async-done(((bf16[2,3,180,1024]{3,2,1,0:T(8,128)(2,1)}), bf16[2,3,180,256]{3,2,1,0:T(8,128)(2,1)}) %reduce-scatter.5.cloned.1.call-update) | async-done | bytes 552976 | tf_op jit(solution)/shard_map/reduce_scatter | solution.py:153
  233.6 33.3 %reduce-scatter.3.cloned.1.call-done = bf16[2,3,180,256]{3,2,1,0:T(8,128)(2,1)} async-done(((bf16[2,3,180,1024]{3,2,1,0:T(8,128)(2,1)}), bf16[2,3,180,256]{3,2,1,0:T(8,128)(2,1)}) %reduce-scatter.3.cloned.1.call-update) | async-done | bytes 552976 | tf_op jit(solution)/shard_map/reduce_scatter | solution.py:153
  271.7 7.6 %all-to-all-start.7 = ((f32[2,2,3,96,128]{4,1,2,0,3:T(2,128)}), f32[2,2,3,96,128]{4,1,2,0,3:T(2,128)S(1)}, u32[]{:S(2)}, u32[]{:S(2)}) async-start(f32[2,2,3,96,128]{4,1,2,0,3:T(2,128)} %copy.198), calls=%async_computation.9 | async-start | bytes 1179648 | tf_op jit(solution)/shard_map/all_to_all | solution.py:99
  281.6 9.6 %all-to-all-done.7 = f32[2,2,3,96,128]{4,1,2,0,3:T(2,128)S(1)} async-done(((f32[2,2,3,96,128]{4,1,2,0,3:T(2,128)}), f32[2,2,3,96,128]{4,1,2,0,3:T(2,128)S(1)}, u32[]{:S(2)}, u32[]{:S(2)}) %all-to-all-start.7) | async-done | bytes 589856 | tf_op jit(solution)/shard_map/all_to_all | solution.py:99
  291.2 4.1 %all-to-all-start.5 = ((f32[2,2,3,96,128]{4,1,2,0,3:T(2,128)}), f32[2,2,3,96,128]{4,1,2,0,3:T(2,128)S(1)}, u32[]{:S(2)}, u32[]{:S(2)}) async-start(f32[2,2,3,96,128]{4,1,2,0,3:T(2,128)} %copy.184), calls=%async_computation.7 | async-start | bytes 1179648 | tf_op jit(solution)/shard_map/all_to_all | solution.py:99
  297.2 9.9 %all-to-all-done.5 = f32[2,2,3,96,128]{4,1,2,0,3:T(2,128)S(1)} async-done(((f32[2,2,3,96,128]{4,1,2,0,3:T(2,128)}), f32[2,2,3,96,128]{4,1,2,0,3:T(2,128)S(1)}, u32[]{:S(2)}, u32[]{:S(2)}) %all-to-all-start.5) | async-done | bytes 589856 | tf_op jit(solution)/shard_map/all_to_all | solution.py:99
  317.6 4.9 %all-to-all-start.6 = ((f32[2,2,96,3,128]{4,1,3,0,2:T(2,128)}), f32[2,2,96,3,128]{4,1,3,0,2:T(2,128)}, u32[]{:S(2)}, u32[]{:S(2)}) async-start(f32[2,2,96,3,128]{4,1,3,0,2:T(2,128)} %copy.192), calls=%async_computation.8 | async-start | bytes 1179648 | tf_op jit(solution)/shard_map/all_to_all | solution.py:105
  334.3 7.0 %all-to-all-start.8 = ((f32[2,2,96,3,128]{4,1,3,0,2:T(2,128)}), f32[2,2,96,3,128]{4,1,3,0,2:T(2,128)S(1)}, u32[]{:S(2)}, u32[]{:S(2)}) async-start(f32[2,2,96,3,128]{4,1,3,0,2:T(2,128)} %copy.206), calls=%async_computation.10 | async-start | bytes 1179648 | tf_op jit(solution)/shard_map/all_to_all | solution.py:105
  343.5 9.5 %all-to-all-done.8 = f32[2,2,96,3,128]{4,1,3,0,2:T(2,128)S(1)} async-done(((f32[2,2,96,3,128]{4,1,3,0,2:T(2,128)}), f32[2,2,96,3,128]{4,1,3,0,2:T(2,128)S(1)}, u32[]{:S(2)}, u32[]{:S(2)}) %all-to-all-start.8) | async-done | bytes 589856 | tf_op jit(solution)/shard_map/all_to_all | solution.py:105
  356.7 3.5 collective-permute-done.7
  363.0 2.6 collective-permute-done.8
  (274 shorter events, 103.2 us)
Async XLA Ops:
  7.2 183.0 %copy-start = (bf16[1024,1024]{1,0:T(8,128)(2,1)S(1)}, bf16[1024,1024]{1,0:T(8,128)(2,1)}, u32[]{:S(2)}) copy-start(bf16[1024,1024]{1,0:T(8,128)(2,1)} %param.14) | copy-start | bytes 6291460
  7.2 94.4 %collective-permute-start.4 = (bf16[2,3,180,256]{3,0,2,1:T(2,128)(2,1)}, bf16[2,3,180,256]{3,0,2,1:T(2,128)(2,1)}, u32[]{:S(2)}, u32[]{:S(2)}) collective-permute-start(bf16[2,3,180,256]{3,0,2,1:T(2,128)(2,1)} %param.9), channel_id=1, source_target_pairs={{0,3},{1,0},{2,1},{3,2},{4,7},{5,4},{6,5},{7,6},{8,11},{9,8},{10,9... | collective-permute-start | bytes 1658888 | tf_op jit(solution)/shard_map/ppermute | solution.py:135
  10.3 91.3 %collective-permute-start.3 = (bf16[2,3,180,256]{3,0,2,1:T(2,128)(2,1)}, bf16[2,3,180,256]{3,0,2,1:T(2,128)(2,1)}, u32[]{:S(2)}, u32[]{:S(2)}) collective-permute-start(bf16[2,3,180,256]{3,0,2,1:T(2,128)(2,1)} %param.9), channel_id=1, source_target_pairs={{0,2},{1,3},{2,0},{3,1},{4,6},{5,7},{6,4},{7,5},{8,10},{9,11},{10,... | collective-permute-start | bytes 1658888 | tf_op jit(solution)/shard_map/ppermute | solution.py:135
  11.0 90.7 %collective-permute-start.2 = (bf16[2,3,180,256]{3,0,2,1:T(2,128)(2,1)}, bf16[2,3,180,256]{3,0,2,1:T(2,128)(2,1)}, u32[]{:S(2)}, u32[]{:S(2)}) collective-permute-start(bf16[2,3,180,256]{3,0,2,1:T(2,128)(2,1)} %param.9), channel_id=1, source_target_pairs={{0,1},{1,2},{2,3},{3,0},{4,5},{5,6},{6,7},{7,4},{8,9},{9,10},{10,1... | collective-permute-start | bytes 1658888 | tf_op jit(solution)/shard_map/ppermute | solution.py:135
  13.5 21.4 %collective-permute-start = (f32[2,2,3,180]{3,2,1,0:T(4,128)S(1)}, f32[2,2,3,180]{3,2,1,0:T(4,128)S(1)}, u32[]{:S(2)}, u32[]{:S(2)}) collective-permute-start(f32[2,2,3,180]{3,2,1,0:T(4,128)S(1)} %pad_maximum_fusion.8), channel_id=1, source_target_pairs={{0,1},{1,0},{2,3},{3,2},{4,5},{5,4},{6,7},{7,6},{8,9},{9,8},{10,11... | collective-permute-start | bytes 25928 | tf_op jit(solution)/shard_map/ppermute | solution.py:127
  17.1 35.8 %copy-start.26 = (f32[180,91]{1,0:T(8,128)}, f32[180,91]{1,0:T(8,128)S(1)}, u32[]{:S(2)}) copy-start(f32[180,91]{1,0:T(8,128)S(1)} %fusion.232) | copy-start | bytes 196564
  35.0 5.3 %collective-permute-start.1 = (f32[2,2,3,180]{3,2,1,0:T(4,128)S(1)}, f32[2,2,3,180]{3,2,1,0:T(4,128)S(1)}, u32[]{:S(2)}, u32[]{:S(2)}) collective-permute-start(f32[2,2,3,180]{3,2,1,0:T(4,128)S(1)} %fusion.551), channel_id=1, source_target_pairs={{0,2},{1,3},{2,0},{3,1},{4,6},{5,7},{6,4},{7,5},{8,10},{9,11},{10,... | collective-permute-start | bytes 25928 | tf_op jit(solution)/shard_map/ppermute | solution.py:127
  38.5 14.9 %copy-start.28 = (f32[180,91]{1,0:T(8,128)}, f32[180,91]{1,0:T(8,128)S(1)}, u32[]{:S(2)}) copy-start(f32[180,91]{1,0:T(8,128)S(1)} %fusion.228) | copy-start | bytes 196564
  42.2 10.1 %copy-start.46 = (f32[2,256]{1,0:T(2,128)S(1)}, f32[2,256]{1,0:T(2,128)}, u32[]{:S(2)}) copy-start(f32[2,256]{1,0:T(2,128)} %param.13) | copy-start | bytes 6148
  44.0 20.1 %all-to-all-start = ((f32[2,2,3,96,128]{4,1,2,0,3:T(2,128)}), f32[2,2,3,96,128]{4,1,2,0,3:T(2,128)}, u32[]{:S(2)}, u32[]{:S(2)}) async-start(f32[2,2,3,96,128]{4,1,2,0,3:T(2,128)} %copy.149), calls=%async_computation | async-start | bytes 1179648 | tf_op jit(solution)/shard_map/all_to_all | solution.py:99
  64.1 16.0 %all-to-all-start.2 = ((f32[2,2,3,96,128]{4,1,2,0,3:T(2,128)}), f32[2,2,3,96,128]{4,1,2,0,3:T(2,128)S(1)}, u32[]{:S(2)}, u32[]{:S(2)}) async-start(f32[2,2,3,96,128]{4,1,2,0,3:T(2,128)} %copy.163), calls=%async_computation.2 | async-start | bytes 1179648 | tf_op jit(solution)/shard_map/all_to_all | solution.py:99
  92.2 16.4 %all-to-all-start.1 = ((f32[2,2,96,3,128]{4,1,3,0,2:T(2,128)}), f32[2,2,96,3,128]{4,1,3,0,2:T(2,128)}, u32[]{:S(2)}, u32[]{:S(2)}) async-start(f32[2,2,96,3,128]{4,1,3,0,2:T(2,128)} %copy.157), calls=%async_computation.1 | async-start | bytes 1179648 | tf_op jit(solution)/shard_map/all_to_all | solution.py:105
  108.5 16.0 %all-to-all-start.3 = ((f32[2,2,96,3,128]{4,1,3,0,2:T(2,128)}), f32[2,2,96,3,128]{4,1,3,0,2:T(2,128)S(1)}, u32[]{:S(2)}, u32[]{:S(2)}) async-start(f32[2,2,96,3,128]{4,1,3,0,2:T(2,128)} %copy.171), calls=%async_computation.3 | async-start | bytes 1179648 | tf_op jit(solution)/shard_map/all_to_all | solution.py:105
  113.1 13.0 %copy-start.30 = (f32[180,91]{1,0:T(8,128)}, f32[180,91]{1,0:T(8,128)S(1)}, u32[]{:S(2)}) copy-start(f32[180,91]{1,0:T(8,128)S(1)} %get-tuple-element.64) | copy-start | bytes 196564
  113.1 14.2 %copy-start.32 = (f32[180,91]{1,0:T(8,128)}, f32[180,91]{1,0:T(8,128)S(1)}, u32[]{:S(2)}) copy-start(f32[180,91]{1,0:T(8,128)S(1)} %get-tuple-element.63) | copy-start | bytes 196564
  134.6 44.2 %all-to-all-start.4 = ((bf16[2,3,180,1024]{2,0,1,3:T(2,128)(2,1)}), bf16[2,3,180,1024]{2,0,1,3:T(2,128)(2,1)}, u32[]{:S(2)}, u32[]{:S(2)}) async-start(bf16[2,3,180,1024]{2,0,1,3:T(2,128)(2,1)} %bitcast.632), calls=%async_computation.4 | async-start | bytes 6291456 | tf_op jit(solution)/shard_map/all_to_all | solution.py:231
  140.0 93.5 %reduce-scatter.5.cloned.1.call-start = ((), (), s32[]{:S(2)}) async-start(), calls=%async_computation.12 | async-start | bytes 2826240 | tf_op jit(solution)/shard_map/reduce_scatter | solution.py:153
  206.2 60.7 %reduce-scatter.3.cloned.1.call-start = ((), (), s32[]{:S(2)}) async-start(), calls=%async_computation.11 | async-start | bytes 2826240 | tf_op jit(solution)/shard_map/reduce_scatter | solution.py:153
  213.9 53.0 %copy-start.6 = (bf16[2,3,180,256]{3,2,1,0:T(8,128)(2,1)S(1)}, bf16[2,3,180,256]{3,2,1,0:T(8,128)(2,1)}, u32[]{:S(2)}) copy-start(bf16[2,3,180,256]{3,2,1,0:T(8,128)(2,1)} %copy-done.5) | copy-start | bytes 1658884
  213.9 53.0 %copy-start.36 = (bf16[2,3,180,256]{3,0,2,1:T(2,128)(2,1)S(1)}, bf16[2,3,180,256]{3,0,2,1:T(2,128)(2,1)}, u32[]{:S(2)}) copy-start(bf16[2,3,180,256]{3,0,2,1:T(2,128)(2,1)} %param.9) | copy-start | bytes 1658884
  214.0 55.4 %copy-start.33 = (f32[180,91]{1,0:T(8,128)S(1)}, f32[180,91]{1,0:T(8,128)}, u32[]{:S(2)}) copy-start(f32[180,91]{1,0:T(8,128)} %copy-done.32) | copy-start | bytes 196564
  214.0 4.1 %collective-permute-start.5 = (f32[2,2,3,180]{3,2,1,0:T(4,128)S(1)}, f32[2,2,3,180]{3,2,1,0:T(4,128)S(1)}, u32[]{:S(2)}, u32[]{:S(2)}) collective-permute-start(f32[2,2,3,180]{3,2,1,0:T(4,128)S(1)} %pad_maximum_fusion.9), channel_id=1, source_target_pairs={{0,1},{1,0},{2,3},{3,2},{4,5},{5,4},{6,7},{7,6},{8,9},{9,8},{10,11... | collective-permute-start | bytes 25928 | tf_op jit(solution)/shard_map/ppermute | solution.py:127
  218.1 5.8 %collective-permute-start.6 = (f32[2,2,3,180]{3,2,1,0:T(4,128)S(1)}, f32[2,2,3,180]{3,2,1,0:T(4,128)S(1)}, u32[]{:S(2)}, u32[]{:S(2)}) collective-permute-start(f32[2,2,3,180]{3,2,1,0:T(4,128)S(1)} %fusion.550), channel_id=1, source_target_pairs={{0,2},{1,3},{2,0},{3,1},{4,6},{5,7},{6,4},{7,5},{8,10},{9,11},{10,... | collective-permute-start | bytes 25928 | tf_op jit(solution)/shard_map/ppermute | solution.py:127
  271.7 19.5 %all-to-all-start.7 = ((f32[2,2,3,96,128]{4,1,2,0,3:T(2,128)}), f32[2,2,3,96,128]{4,1,2,0,3:T(2,128)S(1)}, u32[]{:S(2)}, u32[]{:S(2)}) async-start(f32[2,2,3,96,128]{4,1,2,0,3:T(2,128)} %copy.198), calls=%async_computation.9 | async-start | bytes 1179648 | tf_op jit(solution)/shard_map/all_to_all | solution.py:99
  291.2 15.9 %all-to-all-start.5 = ((f32[2,2,3,96,128]{4,1,2,0,3:T(2,128)}), f32[2,2,3,96,128]{4,1,2,0,3:T(2,128)S(1)}, u32[]{:S(2)}, u32[]{:S(2)}) async-start(f32[2,2,3,96,128]{4,1,2,0,3:T(2,128)} %copy.184), calls=%async_computation.7 | async-start | bytes 1179648 | tf_op jit(solution)/shard_map/all_to_all | solution.py:99
  297.2 11.8 %copy-start.20 = (f32[2,96,3,1,128]{4,1,2,0,3:T(8,128)S(1)}, f32[2,96,3,1,128]{4,1,2,0,3:T(8,128)}, u32[]{:S(2)}) copy-start(f32[2,96,3,1,128]{4,1,2,0,3:T(8,128)} %copy-done.19) | copy-start | bytes 884740
  317.6 16.7 %all-to-all-start.6 = ((f32[2,2,96,3,128]{4,1,3,0,2:T(2,128)}), f32[2,2,96,3,128]{4,1,3,0,2:T(2,128)}, u32[]{:S(2)}, u32[]{:S(2)}) async-start(f32[2,2,96,3,128]{4,1,3,0,2:T(2,128)} %copy.192), calls=%async_computation.8 | async-start | bytes 1179648 | tf_op jit(solution)/shard_map/all_to_all | solution.py:105
  333.4 9.5 %copy-start.29 = (f32[180,91]{1,0:T(8,128)S(1)}, f32[180,91]{1,0:T(8,128)}, u32[]{:S(2)}) copy-start(f32[180,91]{1,0:T(8,128)} %copy-done.28) | copy-start | bytes 196564
  334.3 18.8 %all-to-all-start.8 = ((f32[2,2,96,3,128]{4,1,3,0,2:T(2,128)}), f32[2,2,96,3,128]{4,1,3,0,2:T(2,128)S(1)}, u32[]{:S(2)}, u32[]{:S(2)}) async-start(f32[2,2,96,3,128]{4,1,3,0,2:T(2,128)} %copy.206), calls=%async_computation.10 | async-start | bytes 1179648 | tf_op jit(solution)/shard_map/all_to_all | solution.py:105
  343.5 10.8 %copy-start.27 = (f32[180,91]{1,0:T(8,128)S(1)}, f32[180,91]{1,0:T(8,128)}, u32[]{:S(2)}) copy-start(f32[180,91]{1,0:T(8,128)} %copy-done.26) | copy-start | bytes 196564
  356.4 3.8 %collective-permute-start.7 = (f32[2,2,3,180]{3,2,1,0:T(4,128)S(1)}, f32[2,2,3,180]{3,2,1,0:T(4,128)S(1)}, u32[]{:S(2)}, u32[]{:S(2)}) collective-permute-start(f32[2,2,3,180]{3,2,1,0:T(4,128)S(1)} %pad_maximum_fusion.10), channel_id=1, source_target_pairs={{0,1},{1,0},{2,3},{3,2},{4,5},{5,4},{6,7},{7,6},{8,9},{9,8},{10,11... | collective-permute-start | bytes 25928 | tf_op jit(solution)/shard_map/ppermute | solution.py:127
  360.2 5.3 %collective-permute-start.8 = (f32[2,2,3,180]{3,2,1,0:T(4,128)S(1)}, f32[2,2,3,180]{3,2,1,0:T(4,128)S(1)}, u32[]{:S(2)}, u32[]{:S(2)}) collective-permute-start(f32[2,2,3,180]{3,2,1,0:T(4,128)S(1)} %fusion.549), channel_id=1, source_target_pairs={{0,2},{1,3},{2,0},{3,1},{4,6},{5,7},{6,4},{7,5},{8,10},{9,11},{10,... | collective-permute-start | bytes 25928 | tf_op jit(solution)/shard_map/ppermute | solution.py:127
  (36 other events, 115.8 us)
Sparse Core Ops, SparseCore 0:
  206.3 27.1 reduce-scatter.4
  236.1 30.7 reduce-scatter.2
